TPU v7x, 32 devices: a whole 2x2x4 slice. The times are simulated.
32 devices in a mesh: groups: 2 (over y), fsdp: 4 (over z), segment: 4 (over x, core).
Axes of the slice: x: 2, y: 2, z: 4, core: 2. Of those that a mesh axis runs over, the one named last changes fastest.
Arguments:
- layer_inputs: bfloat16 [32, 8192], P(('groups', 'fsdp'), 'segment'), parts along dimension 0, may hold values from -6 to 6
- labels: int32 [32], P('groups'), parts along dimension 0, may hold values from 0 to 1
- head_weight: float32 [4096], replicated, may hold values from -5 to 5
- gate_up_store: bfloat16 [1280, 4, 2, 128, 128], P('fsdp', 'segment'), may hold values from -0.125 to 0.125
- down_store: bfloat16 [1280, 4, 128, 128], P('fsdp', 'segment'), may hold values from -0.0625 to 0.0625
- kept_rows: int32 [2, 128, 16], replicated, may hold values from 0 to 31, as said below
- owners: int32 [2, 128, 16], replicated, may hold values from 0 to 3, as said below
- slots: int32 [2, 128, 16], replicated, may hold values from 0 to 319, as said below
Outputs:
- input_grads: bfloat16 [32, 8192], P(('groups', 'fsdp'), 'segment'), parts along dimension 0
- gate_up_grads: bfloat16 [2560, 4, 2, 128, 128], P(('groups', 'fsdp'), 'segment'), parts along dimension 0
- down_grads: bfloat16 [2560, 4, 128, 128], P(('groups', 'fsdp'), 'segment'), parts along dimension 0
There are 2 independent parts, one for each index of `groups`. A program takes and returns all parts, laid end to end along the dimension named above; an argument that names none is the same for every part. Nothing has to cross between parts.
Inputs may be any that keep to these rules, and one draw needn't show every extreme that they name: kept_rows[p, j] holds 16 distinct block rows. `owners`: call (j // 16) mod 4 the reader of hidden block column j. For each segment p and each value of j // 64, one fsdp index stores at most 320 of those kept blocks, and at most 80 of them with one reader; both bounds are reached. Kept blocks with the same segment, the same j // 64 and the same owner have distinct slots.
All inputs are finite; a program needn't handle non-finite values.
Results may differ from a plain program's by a relative error of at most 0.008.
Values may be sent and summed in bfloat16 or wider, within the bound.
No kernel may reach another device: no remote copies, remote signals or barrier semaphores. Data moves between devices by JAX's collectives and lax.ppermute only.
A program may use at most 256 MiB of HBM per device.

v0:
```python
import jax
import jax.numpy as jnp
from jax import lax
from jax.sharding import PartitionSpec as P

PIPE = 2
HI = lax.Precision.HIGHEST


def per_device(
    layer_inputs, labels, head_weight, gate_up_store, down_store, kept_rows, owners, slots
):
    members = lax.axis_size("fsdp")
    places = lax.axis_size("segment")
    sections = places // PIPE
    member = lax.axis_index("fsdp")
    place = lax.axis_index("segment")
    segment = place // sections
    section = place % sections
    is_last = segment == PIPE - 1
    tok_rows, piece_width = layer_inputs.shape
    tokens = tok_rows * members
    width = piece_width * sections
    blk = gate_up_store.shape[-1]
    capacity = gate_up_store.shape[0]
    kept = kept_rows.shape[2]
    sec_cols = kept_rows.shape[1] // sections
    nrow = width // blk
    nblocks = sec_cols * kept
    first_col = section * sec_cols
    sec_rows = lax.dynamic_slice(kept_rows, (segment, first_col, 0), (1, sec_cols, kept))
    sec_owner = lax.dynamic_slice(owners, (segment, first_col, 0), (1, sec_cols, kept))
    sec_slot = lax.dynamic_slice(slots, (segment, first_col, 0), (1, sec_cols, kept))
    sec_rows = sec_rows.reshape(nblocks)
    mine = sec_owner.reshape(nblocks) == member
    block_col = jnp.arange(nblocks, dtype=jnp.int32) // kept
    hits = mine[None, :] & (
        sec_slot.reshape(nblocks)[None, :] == jnp.arange(capacity, dtype=jnp.int32)[:, None]
    )
    valid = jnp.any(hits, axis=1)
    slot_col = jnp.sum(jnp.where(hits, block_col[None, :], 0), axis=1)
    slot_row = jnp.sum(jnp.where(hits, sec_rows[None, :], 0), axis=1)
    col_hot = valid[:, None] & (slot_col[:, None] == jnp.arange(sec_cols, dtype=jnp.int32)[None, :])
    row_hot = valid[:, None] & (slot_row[:, None] == jnp.arange(nrow, dtype=jnp.int32)[None, :])
    col_f = col_hot.astype(jnp.float32)
    col_b = col_hot.astype(jnp.bfloat16)
    row_f = row_hot.astype(jnp.float32)
    row_b = row_hot.astype(jnp.bfloat16)
    w_pair = gate_up_store[:, 0]
    w_down = down_store[:, 0]
    gathered = lax.all_gather(layer_inputs, ("fsdp", "segment"))
    gathered = gathered.reshape(members, places, tok_rows, piece_width)
    x_all = gathered.transpose(0, 2, 1, 3).reshape(tokens, places * piece_width)
    x_mine = lax.dynamic_slice_in_dim(x_all, segment * width, width, axis=1)
    x_last = x_all[:, (PIPE - 1) * width :]
    x_sel = jnp.einsum("cr,trb->ctb", row_b, x_mine.reshape(tokens, nrow, blk))
    x_sel = x_sel.astype(jnp.bfloat16)
    gu_slot = jnp.einsum("cta,cgab->ctgb", x_sel, w_pair, preferred_element_type=jnp.float32)
    gu_part = jnp.einsum("cj,ctgb->gtjb", col_f, gu_slot, precision=HI)
    head_rows = head_weight.reshape(nrow, blk)
    head_sel = jnp.einsum("cr,rd->cd", row_f, head_rows, precision=HI)
    folded = jnp.einsum("chd,cd->ch", w_down.astype(jnp.float32), head_sel, precision=HI)
    f_part = jnp.einsum("cj,ch->jh", col_f, folded, precision=HI)
    packed = jnp.concatenate([gu_part.reshape(2 * tokens, sec_cols, blk), f_part[None]], axis=0)
    packed = lax.psum(packed, "fsdp")
    gate = packed[:tokens]
    up = packed[tokens : 2 * tokens]
    f_sum = packed[2 * tokens]
    sig = jax.nn.sigmoid(gate)
    hidden = (gate * sig * up).astype(jnp.bfloat16)
    branch = jnp.einsum("tjh,jh->t", hidden.astype(jnp.float32), f_sum, precision=HI)
    branch = jnp.where(is_last, branch, 0.0)
    branch = lax.psum(branch, "segment")
    x_term = jnp.einsum("td,d->t", x_last.astype(jnp.float32), head_weight, precision=HI)
    logits = (x_term + branch) * width ** (-0.5)
    dlogit = jax.nn.sigmoid(logits) - labels.astype(jnp.float32)
    dout_last = (dlogit[:, None] * head_weight[None, :]).astype(jnp.bfloat16)

    def gate_grads(dhidden):
        dgate = (dhidden * up * sig * (1.0 + gate * (1.0 - sig))).astype(jnp.bfloat16)
        dup = (dhidden * gate * sig).astype(jnp.bfloat16)
        pair = jnp.stack([dgate, dup], axis=2)
        return jnp.einsum("cj,tjgb->ctgb", col_b, pair).astype(jnp.bfloat16)

    def spread_rows(d_sel):
        spread = jnp.einsum("ctgb,cgab->cta", d_sel, w_pair, preferred_element_type=jnp.float32)
        return jnp.einsum("cr,cta->tra", row_f, spread, precision=HI).reshape(tokens, width)

    d_sel_last = gate_grads(dlogit[:, None, None] * f_sum[None])
    part_last = jnp.where(is_last, spread_rows(d_sel_last), 0.0)
    sum_last = lax.psum(part_last, ("fsdp", "segment"))
    grad_last = (dout_last.astype(jnp.float32) + sum_last).astype(jnp.bfloat16)
    dout_sel = jnp.einsum("cr,trd->ctd", row_b, grad_last.reshape(tokens, nrow, blk))
    dout_sel = dout_sel.astype(jnp.bfloat16)
    dh_slot = jnp.einsum("ctd,chd->cth", dout_sel, w_down, preferred_element_type=jnp.float32)
    dh_part = jnp.einsum("cj,cth->tjh", col_f, dh_slot, precision=HI)
    dhidden_first = lax.psum(dh_part, "fsdp")
    d_sel_first = gate_grads(dhidden_first)
    part_first = jnp.where(is_last, 0.0, spread_rows(d_sel_first))
    sum_first = lax.psum(part_first, ("fsdp", "segment"))
    grad_first = (grad_last.astype(jnp.float32) + sum_first).astype(jnp.bfloat16)
    rows_at = member * tok_rows
    cols_at = section * piece_width
    grads = jnp.where(is_last, grad_last, grad_first)
    input_grads = lax.dynamic_slice(grads, (rows_at, cols_at), (tok_rows, piece_width))
    d_sel = jnp.where(is_last, d_sel_last, d_sel_first)
    cot_sel = jnp.where(
        is_last,
        jnp.einsum("cr,trd->ctd", row_b, dout_last.reshape(tokens, nrow, blk)).astype(jnp.bfloat16),
        dout_sel,
    )
    hid_sel = jnp.einsum("cj,tjh->cth", col_b, hidden).astype(jnp.bfloat16)
    grad_pair = jnp.einsum(
        "cta,ctgb->cgab", x_sel, d_sel, preferred_element_type=jnp.float32
    ).astype(jnp.bfloat16)
    grad_down = jnp.einsum(
        "cth,ctd->chd", hid_sel, cot_sel, preferred_element_type=jnp.float32
    ).astype(jnp.bfloat16)
    zero_bf = jnp.zeros((), jnp.bfloat16)
    grad_pair = jnp.where(valid[:, None, None, None], grad_pair, zero_bf)
    grad_down = jnp.where(valid[:, None, None], grad_down, zero_bf)
    return (input_grads, grad_pair[:, None], grad_down[:, None])


def solution(mesh):
    return jax.shard_map(
        per_device,
        mesh=mesh,
        in_specs=(
            P(("groups", "fsdp"), "segment"),
            P("groups"),
            P(),
            P("fsdp", "segment", None, None, None),
            P("fsdp", "segment", None, None),
            P(),
            P(),
            P(),
        ),
        out_specs=(
            P(("groups", "fsdp"), "segment"),
            P(("groups", "fsdp"), "segment", None, None, None),
            P(("groups", "fsdp"), "segment", None, None),
        ),
        check_vma=False,
    )
```

profile of v0, /device:TPU:1, one launch (start us, length us, event | category | flops | bytes accessed | tf_op | source)
XLA Modules:
  0.0 401.1 jit_solution(11632360739966436155)
XLA Ops:
  9.3 23.9 %all-gather.1 = bf16[16,4,2048]{2,1,0:T(4,128)(2,1)S(1)} all-gather(bf16[1,4,2048]{2,1,0:T(4,128)(2,1)} %bitcast.150), channel_id=2, replica_groups=mesh['groups'=2,'fsdp'=4,'segment'=4] {'fsdp','segment'}, dimensions={0}, use_global_device_ids=true | all-gather | bytes 278528 | tf_op jit(solution)/shard_map/all_gather | solution.py:51
  36.2 19.3 %fusion.8 = f32[320,1,128]{2,1,0:T(1,128)S(1)} fusion(f32[320,128,1]{1,2,0:T(1,128)S(1)} %bitcast.141, bf16[320,1,128,128]{3,2,1,0:T(8,128)(2,1)} %param.12), kind=kOutput, calls=%fused_computation.9 | convolution fusion | flops 62914560 | bytes 10813440 | tf_op jit(solution)/shard_map/chd,cd->ch/dot_general | solution.py:62
  55.8 9.1 %fusion.4 = f32[320,16,2,128]{3,1,2,0:T(8,128)S(1)} fusion(bf16[320,1,2,128,128]{4,3,2,1,0:T(8,128)(2,1)} %param.11, bf16[320,16,128,1]{2,0,1,3:T(8,128)(2,1)S(1)} %convolution_bitcast_fusion), kind=kOutput, calls=%fused_computation.4 | convolution fusion | flops 335544320 | bytes 27525120 | tf_op jit(solution)/shard_map/cta,cgab->ctgb/dot_general | solution.py:58
  64.9 5.3 %fusion.31 = f32[2,16,64,128]{3,2,0,1:T(8,128)S(1)} fusion(f32[320,16,2,128]{3,1,2,0:T(8,128)S(1)} %fusion.4, s32[320]{0:T(512)S(1)} %get-tuple-element.15, pred[320]{0:T(512)(128)(4,1)S(1)} %fusion.38), kind=kOutput, calls=%fused_computation.28 | convolution fusion | flops 1006673920 | bytes 6293056 | tf_op jit(solution)/shard_map/cj,ctgb->gtjb/dot_general | solution.py:59
  71.4 49.9 %all-reduce.5.cloned.1.call-done = f32[33,64,128]{2,1,0:T(8,128)} async-done(((f32[33,64,128]{2,1,0:T(8,128)}), f32[33,64,128]{2,1,0:T(8,128)}) %all-reduce.5.cloned.1.call-update) | async-done | bytes 1081360 | tf_op jit(solution)/shard_map/psum | solution.py:65
  122.2 1.3 multiply_convert_fusion.2
  124.1 6.0 %psum.36 = f32[16]{0:T(128)S(1)} all-reduce(f32[16]{0:T(128)S(1)} %fusion.50), channel_id=1, replica_groups=mesh['groups'=2,'fsdp'=4,'segment'=4] {'segment'}, use_global_device_ids=true, to_apply=%region_4.5 | all-reduce | flops 16 | bytes 128 | tf_op jit(solution)/shard_map/psum | solution.py:73
  131.6 10.8 %fusion.21 = f32[320,16,128]{2,1,0:T(8,128)S(1)} fusion(bf16[320,1,2,128,128]{4,3,2,1,0:T(8,128)(2,1)} %param.11, bf16[320,16,2,128]{3,0,2,1:T(8,128)(2,1)S(1)} %fusion.63), kind=kOutput, calls=%fused_computation.24 | convolution fusion | flops 335544320 | bytes 26214400 | tf_op jit(solution)/shard_map/ctgb,cgab->cta/dot_general | solution.py:86
  142.3 1.8 fusion.42
  145.0 1.6 fusion.81
  146.6 87.7 %all-reduce.7.cloned.1.call-done = f32[16,4096]{1,0:T(8,128)} async-done(((f32[16,4096]{1,0:T(8,128)}), f32[16,4096]{1,0:T(8,128)}) %all-reduce.7.cloned.1.call-update) | async-done | bytes 262160 | tf_op jit(solution)/shard_map/psum | solution.py:91
  236.0 8.7 %fusion.6 = f32[320,16,128]{2,1,0:T(8,128)S(1)} fusion(bf16[320,1,128,128]{3,2,1,0:T(8,128)(2,1)} %param.12, bf16[320,16,128]{2,0,1:T(8,128)(2,1)S(1)} %fusion.114), kind=kOutput, calls=%fused_computation.7 | convolution fusion | flops 167772160 | bytes 14417920 | tf_op jit(solution)/shard_map/ctd,chd->cth/dot_general | solution.py:95
  244.7 2.7 fusion.39
  247.6 2.0 convolution_select_fusion
  249.6 10.0 %select_bitcast_fusion.1 = bf16[320,1,128,128]{3,2,1,0:T(8,128)(2,1)} fusion(pred[320]{0:T(512)(128)(4,1)S(1)} %fusion.38, bf16[320,16,128]{2,0,1:T(8,128)(2,1)S(1)} %convolution_select_fusion, bf16[320,16,128]{2,0,1:T(8,128)(2,1)S(1)} %copy-done.4), kind=kOutput, calls=%fused_computation.11 | convolution fusion | flops 178257920 | bytes 13107520 | tf_op jit(solution)/shard_map/cth,ctd->chd/dot_general | solution.py:116
  259.7 25.1 %all-reduce.9.cloned.1.call-done = f32[16,64,128]{2,1,0:T(8,128)} async-done(((f32[16,64,128]{2,1,0:T(8,128)}), f32[16,64,128]{2,1,0:T(8,128)}) %all-reduce.9.cloned.1.call-update) | async-done | bytes 524304 | tf_op jit(solution)/shard_map/psum | solution.py:97
  284.7 1.6 fusion.69
  286.4 2.4 broadcast_select_fusion
  288.8 10.8 %fusion.26 = f32[320,16,128]{2,1,0:T(8,128)S(1)} fusion(bf16[320,1,2,128,128]{4,3,2,1,0:T(8,128)(2,1)} %param.11, bf16[320,16,2,128]{3,0,2,1:T(8,128)(2,1)S(1)} %get-tuple-element.24), kind=kOutput, calls=%fused_computation.25 | convolution fusion | flops 335544320 | bytes 26214400 | tf_op jit(solution)/shard_map/ctgb,cgab->cta/dot_general | solution.py:86
  299.5 1.8 fusion.45
  302.2 16.9 %select_bitcast_fusion = bf16[320,1,2,128,128]{3,4,2,0,1:T(8,128)(2,1)} fusion(pred[320]{0:T(512)(128)(4,1)S(1)} %fusion.38, bf16[320,16,2,128]{3,0,2,1:T(8,128)(2,1)} %get-tuple-element.23, bf16[320,16,128,1]{2,0,1,3:T(8,128)(2,1)S(1)} %copy-done.3), kind=kOutput, calls=%fused_computation.6 | convolution fusion | flops 356515840 | bytes 24904000 | tf_op jit(solution)/shard_map/cta,ctgb->cgab/dot_general | solution.py:113
  319.0 27.9 %copy.71 = bf16[320,1,2,128,128]{4,3,2,1,0:T(8,128)(2,1)} copy(bf16[320,1,2,128,128]{3,4,2,0,1:T(8,128)(2,1)} %select_bitcast_fusion) | data formatting | bytes 41943040
  347.0 45.8 %all-reduce.11.cloned.1.call-done = f32[16,4096]{1,0:T(8,128)} async-done(((f32[16,4096]{1,0:T(8,128)}), f32[16,4096]{1,0:T(8,128)}) %all-reduce.11.cloned.1.call-update) | async-done | bytes 262160 | tf_op jit(solution)/shard_map/psum | solution.py:100
  392.8 1.5 fusion.104
  (55 shorter events, 12.9 us)
Async XLA Ops:
  7.2 114.2 %all-reduce.5.cloned.1.call-start = ((), (), s32[]{:S(2)}) async-start(), calls=%async_computation | async-start | bytes 2162688 | tf_op jit(solution)/shard_map/psum | solution.py:65
  36.2 19.6 %copy-start.2 = (bf16[320,16,128,1]{2,0,1,3:T(8,128)(2,1)}, bf16[320,16,128,1]{2,0,1,3:T(8,128)(2,1)S(1)}, u32[]{:S(2)}) copy-start(bf16[320,16,128,1]{2,0,1,3:T(8,128)(2,1)S(1)} %convolution_bitcast_fusion) | copy-start | bytes 3932164
  70.2 59.8 %copy-start.6 = (f32[4096]{0:T(1024)S(1)}, f32[4096]{0:T(1024)}, u32[]{:S(2)}) copy-start(f32[4096]{0:T(1024)} %param.10) | copy-start | bytes 49156
  70.2 59.8 %copy-start.7 = (s32[16]{0:T(128)S(1)}, s32[16]{0:T(128)}, u32[]{:S(2)}) copy-start(s32[16]{0:T(128)} %param.9) | copy-start | bytes 196
  71.4 163.0 %all-reduce.7.cloned.1.call-start = ((), (), s32[]{:S(2)}) async-start(), calls=%async_computation.1 | async-start | bytes 524288 | tf_op jit(solution)/shard_map/psum | solution.py:91
  121.4 9.0 %copy-start.1 = (f32[33,64,128]{2,1,0:T(8,128)S(1)}, f32[33,64,128]{2,1,0:T(8,128)}, u32[]{:S(2)}) copy-start(f32[33,64,128]{2,1,0:T(8,128)} %all-reduce.5.cloned.1.call-done) | copy-start | bytes 3244036
  145.0 139.8 %all-reduce.9.cloned.1.call-start = ((), (), s32[]{:S(2)}) async-start(), calls=%async_computation.2 | async-start | bytes 1048576 | tf_op jit(solution)/shard_map/psum | solution.py:97
  236.0 8.8 %copy-start = (bf16[320,16,128]{2,0,1:T(8,128)(2,1)}, bf16[320,16,128]{2,0,1:T(8,128)(2,1)S(1)}, u32[]{:S(2)}) copy-start(bf16[320,16,128]{2,0,1:T(8,128)(2,1)S(1)} %fusion.114) | copy-start | bytes 3932164
  244.7 2.8 copy-start.5
  247.5 145.3 %all-reduce.11.cloned.1.call-start = ((), (), s32[]{:S(2)}) async-start(), calls=%async_computation.3 | async-start | bytes 524288 | tf_op jit(solution)/shard_map/psum | solution.py:100
  247.5 2.1 copy-start.4
  299.5 2.7 copy-start.3
Sparse Core Ops, SparseCore 0:
  71.5 49.8 all-reduce.4
  145.1 89.1 all-reduce.6
  247.6 37.0 all-reduce.8
  302.3 90.4 all-reduce.10
where the time goes:
time: 405 us; the launch traced here: 401 us
  waiting for transfers between devices  209 us (52%)
  matrix products  107 us (26%)
  local copies, waits for them, and re-layouts  32.3 us (8%)
  blocking collectives  29.9 us (7%)
  between operations  14.3 us (4%)
  other arithmetic  8.74 us (2%)
    psum x1, waiting for transfers between devices, per_device(): sum_last = lax.psum(part_last, ('fsdp', 'segment'))  87.7 us
    psum x1, waiting for transfers between devices, per_device(): packed = lax.psum(packed, 'fsdp')  49.9 us
    psum x1, waiting for transfers between devices, per_device(): sum_first = lax.psum(part_first, ('fsdp', 'segment'))  45.8 us
    unnamed x23, local copies, waits for them, and re-layouts  29.9 us
    psum x1, waiting for transfers between devices, per_device(): dhidden_first = lax.psum(dh_part, 'fsdp')  25.1 us
    all_gather x1, blocking collectives, per_device(): gathered = lax.all_gather(layer_inputs, ('fsdp', 'segment'))  23.9 us
    dot_general x2, matrix products, spread_rows(): jnp.einsum('ctgb,cgab->cta', d_sel, w_pair, preferred_element_type=jnp.fl...  21.5 us
    dot_general x1, matrix products, per_device(): jnp.einsum('chd,cd->ch', w_down.astype(jnp.float32), head_sel, precision=HI)  19.3 us
  transfers between devices with their start and end apart: 4, of which 4 were waited for; matrix products, arithmetic and copies ran while one was open for 15% of the time, Pallas kernels for 0%

commit v1 on v0

--- a/solution.py
+++ b/solution.py
@@ -5,6 +5,11 @@
 
 PIPE = 2
 HI = lax.Precision.HIGHEST
+
+
+def by_each_axis(value, first, second):
+    inner = lax.psum(value, first)
+    return lax.psum(inner, second)
 
 
 def per_device(
@@ -88,7 +93,7 @@
 
     d_sel_last = gate_grads(dlogit[:, None, None] * f_sum[None])
     part_last = jnp.where(is_last, spread_rows(d_sel_last), 0.0)
-    sum_last = lax.psum(part_last, ("fsdp", "segment"))
+    sum_last = by_each_axis(part_last, "segment", "fsdp")
     grad_last = (dout_last.astype(jnp.float32) + sum_last).astype(jnp.bfloat16)
     dout_sel = jnp.einsum("cr,trd->ctd", row_b, grad_last.reshape(tokens, nrow, blk))
     dout_sel = dout_sel.astype(jnp.bfloat16)

time: 405 us -> 385 us (0.951)
  waiting for transfers between devices: 209 us -> 189 us
    psum x1 -> x2, waiting for transfers between devices: 87.7 us -> 66.5 us  [the longest x1 36.3 us: by_each_axis(): return lax.psum(inner, second)]
  transfers between devices with their start and end apart: 4 -> 5, of which waited for: 4 -> 5; matrix products, arithmetic and copies ran while one was open for 15% -> 15% of each run, Pallas kernels for 0% -> 0%
where the time goes in v1:
time: 385 us; the launch traced here: 381 us
  waiting for transfers between devices  189 us (49%)
  matrix products  107 us (28%)
  local copies, waits for them, and re-layouts  32.4 us (8%)
  blocking collectives  29.9 us (8%)
  between operations  14.3 us (4%)
  other arithmetic  8.74 us (2%)
    psum x1, waiting for transfers between devices, per_device(): packed = lax.psum(packed, 'fsdp')  49.9 us
    psum x1, waiting for transfers between devices, per_device(): sum_first = lax.psum(part_first, ('fsdp', 'segment'))  45.8 us
    psum x1, waiting for transfers between devices, by_each_axis(): return lax.psum(inner, second)  36.3 us
    psum x1, waiting for transfers between devices, by_each_axis(): inner = lax.psum(value, first)  30.3 us
    unnamed x23, local copies, waits for them, and re-layouts  29.9 us
    psum x1, waiting for transfers between devices, per_device(): dhidden_first = lax.psum(dh_part, 'fsdp')  26.4 us
    all_gather x1, blocking collectives, per_device(): gathered = lax.all_gather(layer_inputs, ('fsdp', 'segment'))  23.9 us
    dot_general x2, matrix products, spread_rows(): jnp.einsum('ctgb,cgab->cta', d_sel, w_pair, preferred_element_type=jnp.fl...  21.5 us
  transfers between devices with their start and end apart: 5, of which 5 were waited for; matrix products, arithmetic and copies ran while one was open for 15% of the time, Pallas kernels for 0%

profile of v1, /device:TPU:1, one launch (start us, length us, event | category | flops | bytes accessed | tf_op | source)
XLA Modules:
  0.0 381.3 jit_solution(11271375254940870465)
XLA Ops:
  9.3 23.9 %all-gather.1 = bf16[16,4,2048]{2,1,0:T(4,128)(2,1)S(1)} all-gather(bf16[1,4,2048]{2,1,0:T(4,128)(2,1)} %bitcast.150), channel_id=2, replica_groups=mesh['groups'=2,'fsdp'=4,'segment'=4] {'fsdp','segment'}, dimensions={0}, use_global_device_ids=true | all-gather | bytes 278528 | tf_op jit(solution)/shard_map/all_gather | solution.py:56
  36.2 19.3 %fusion.8 = f32[320,1,128]{2,1,0:T(1,128)S(1)} fusion(f32[320,128,1]{1,2,0:T(1,128)S(1)} %bitcast.141, bf16[320,1,128,128]{3,2,1,0:T(8,128)(2,1)} %param.12), kind=kOutput, calls=%fused_computation.9 | convolution fusion | flops 62914560 | bytes 10813440 | tf_op jit(solution)/shard_map/chd,cd->ch/dot_general | solution.py:67
  55.8 9.1 %fusion.4 = f32[320,16,2,128]{3,1,2,0:T(8,128)S(1)} fusion(bf16[320,1,2,128,128]{4,3,2,1,0:T(8,128)(2,1)} %param.11, bf16[320,16,128,1]{2,0,1,3:T(8,128)(2,1)S(1)} %convolution_bitcast_fusion), kind=kOutput, calls=%fused_computation.4 | convolution fusion | flops 335544320 | bytes 27525120 | tf_op jit(solution)/shard_map/cta,cgab->ctgb/dot_general | solution.py:63
  64.9 5.3 %fusion.31 = f32[2,16,64,128]{3,2,0,1:T(8,128)S(1)} fusion(f32[320,16,2,128]{3,1,2,0:T(8,128)S(1)} %fusion.4, s32[320]{0:T(512)S(1)} %get-tuple-element.15, pred[320]{0:T(512)(128)(4,1)S(1)} %fusion.38), kind=kOutput, calls=%fused_computation.28 | convolution fusion | flops 1006673920 | bytes 6293056 | tf_op jit(solution)/shard_map/cj,ctgb->gtjb/dot_general | solution.py:64
  71.4 49.9 %all-reduce.6.cloned.1.call-done = f32[33,64,128]{2,1,0:T(8,128)} async-done(((f32[33,64,128]{2,1,0:T(8,128)}), f32[33,64,128]{2,1,0:T(8,128)}) %all-reduce.6.cloned.1.call-update) | async-done | bytes 1081360 | tf_op jit(solution)/shard_map/psum | solution.py:70
  124.1 6.0 %psum.43 = f32[16]{0:T(128)S(1)} all-reduce(f32[16]{0:T(128)S(1)} %fusion.50), channel_id=1, replica_groups=mesh['groups'=2,'fsdp'=4,'segment'=4] {'segment'}, use_global_device_ids=true, to_apply=%region_4.5 | all-reduce | flops 16 | bytes 128 | tf_op jit(solution)/shard_map/psum | solution.py:78
  131.6 10.8 %fusion.21 = f32[320,16,128]{2,1,0:T(8,128)S(1)} fusion(bf16[320,1,2,128,128]{4,3,2,1,0:T(8,128)(2,1)} %param.11, bf16[320,16,2,128]{3,0,2,1:T(8,128)(2,1)S(1)} %fusion.63), kind=kOutput, calls=%fused_computation.24 | convolution fusion | flops 335544320 | bytes 26214400 | tf_op jit(solution)/shard_map/ctgb,cgab->cta/dot_general | solution.py:91
  142.3 1.8 fusion.42
  145.0 30.3 %all-reduce.8.cloned.1.call-done = f32[16,4096]{1,0:T(8,128)} async-done(((f32[16,4096]{1,0:T(8,128)}), f32[16,4096]{1,0:T(8,128)}) %all-reduce.8.cloned.1.call-update) | async-done | bytes 262160 | tf_op jit(solution)/shard_map/psum | solution.py:11
  175.4 1.6 fusion.81
  177.0 36.3 %all-reduce.10.cloned.1.call-done = f32[16,4096]{1,0:T(8,128)} async-done(((f32[16,4096]{1,0:T(8,128)}), f32[16,4096]{1,0:T(8,128)}) %all-reduce.10.cloned.1.call-update) | async-done | bytes 262160 | tf_op jit(solution)/shard_map/psum | solution.py:12
  214.9 8.7 %fusion.6 = f32[320,16,128]{2,1,0:T(8,128)S(1)} fusion(bf16[320,1,128,128]{3,2,1,0:T(8,128)(2,1)} %param.12, bf16[320,16,128]{2,0,1:T(8,128)(2,1)S(1)} %fusion.114), kind=kOutput, calls=%fused_computation.7 | convolution fusion | flops 167772160 | bytes 14417920 | tf_op jit(solution)/shard_map/ctd,chd->cth/dot_general | solution.py:100
  223.6 2.7 fusion.39
  226.5 2.0 convolution_select_fusion
  228.5 10.0 %select_bitcast_fusion.1 = bf16[320,1,128,128]{3,2,1,0:T(8,128)(2,1)} fusion(pred[320]{0:T(512)(128)(4,1)S(1)} %fusion.38, bf16[320,16,128]{2,0,1:T(8,128)(2,1)S(1)} %convolution_select_fusion, bf16[320,16,128]{2,0,1:T(8,128)(2,1)S(1)} %copy-done.4), kind=kOutput, calls=%fused_computation.11 | convolution fusion | flops 178257920 | bytes 13107520 | tf_op jit(solution)/shard_map/cth,ctd->chd/dot_general | solution.py:121
  238.6 26.4 %all-reduce.12.cloned.1.call-done = f32[16,64,128]{2,1,0:T(8,128)} async-done(((f32[16,64,128]{2,1,0:T(8,128)}), f32[16,64,128]{2,1,0:T(8,128)}) %all-reduce.12.cloned.1.call-update) | async-done | bytes 524304 | tf_op jit(solution)/shard_map/psum | solution.py:102
  264.9 1.6 fusion.69
  266.6 2.4 broadcast_select_fusion
  269.0 10.8 %fusion.26 = f32[320,16,128]{2,1,0:T(8,128)S(1)} fusion(bf16[320,1,2,128,128]{4,3,2,1,0:T(8,128)(2,1)} %param.11, bf16[320,16,2,128]{3,0,2,1:T(8,128)(2,1)S(1)} %get-tuple-element.24), kind=kOutput, calls=%fused_computation.25 | convolution fusion | flops 335544320 | bytes 26214400 | tf_op jit(solution)/shard_map/ctgb,cgab->cta/dot_general | solution.py:91
  279.7 1.8 fusion.45
  282.4 16.9 %select_bitcast_fusion = bf16[320,1,2,128,128]{3,4,2,0,1:T(8,128)(2,1)} fusion(pred[320]{0:T(512)(128)(4,1)S(1)} %fusion.38, bf16[320,16,2,128]{3,0,2,1:T(8,128)(2,1)} %get-tuple-element.23, bf16[320,16,128,1]{2,0,1,3:T(8,128)(2,1)S(1)} %copy-done.3), kind=kOutput, calls=%fused_computation.6 | convolution fusion | flops 356515840 | bytes 24904000 | tf_op jit(solution)/shard_map/cta,ctgb->cgab/dot_general | solution.py:118
  299.3 27.9 %copy.71 = bf16[320,1,2,128,128]{4,3,2,1,0:T(8,128)(2,1)} copy(bf16[320,1,2,128,128]{3,4,2,0,1:T(8,128)(2,1)} %select_bitcast_fusion) | data formatting | bytes 41943040
  327.2 45.8 %all-reduce.14.cloned.1.call-done = f32[16,4096]{1,0:T(8,128)} async-done(((f32[16,4096]{1,0:T(8,128)}), f32[16,4096]{1,0:T(8,128)}) %all-reduce.14.cloned.1.call-update) | async-done | bytes 262160 | tf_op jit(solution)/shard_map/psum | solution.py:105
  373.0 1.5 fusion.104
  (58 shorter events, 14.3 us)
Async XLA Ops:
  7.2 114.2 %all-reduce.6.cloned.1.call-start = ((), (), s32[]{:S(2)}) async-start(), calls=%async_computation | async-start | bytes 2162688 | tf_op jit(solution)/shard_map/psum | solution.py:70
  36.2 19.6 %copy-start.2 = (bf16[320,16,128,1]{2,0,1,3:T(8,128)(2,1)}, bf16[320,16,128,1]{2,0,1,3:T(8,128)(2,1)S(1)}, u32[]{:S(2)}) copy-start(bf16[320,16,128,1]{2,0,1,3:T(8,128)(2,1)S(1)} %convolution_bitcast_fusion) | copy-start | bytes 3932164
  70.2 59.8 %copy-start.6 = (f32[4096]{0:T(1024)S(1)}, f32[4096]{0:T(1024)}, u32[]{:S(2)}) copy-start(f32[4096]{0:T(1024)} %param.10) | copy-start | bytes 49156
  70.2 59.8 %copy-start.7 = (s32[16]{0:T(128)S(1)}, s32[16]{0:T(128)}, u32[]{:S(2)}) copy-start(s32[16]{0:T(128)} %param.9) | copy-start | bytes 196
  71.4 103.9 %all-reduce.8.cloned.1.call-start = ((), (), s32[]{:S(2)}) async-start(), calls=%async_computation.1 | async-start | bytes 524288 | tf_op jit(solution)/shard_map/psum | solution.py:11
  121.4 9.0 %copy-start.1 = (f32[33,64,128]{2,1,0:T(8,128)S(1)}, f32[33,64,128]{2,1,0:T(8,128)}, u32[]{:S(2)}) copy-start(f32[33,64,128]{2,1,0:T(8,128)} %all-reduce.6.cloned.1.call-done) | copy-start | bytes 3244036
  145.0 68.2 %all-reduce.10.cloned.1.call-start = ((), (), s32[]{:S(2)}) async-start(), calls=%async_computation.2 | async-start | bytes 524288 | tf_op jit(solution)/shard_map/psum | solution.py:12
  175.3 89.6 %all-reduce.12.cloned.1.call-start = ((), (), s32[]{:S(2)}) async-start(), calls=%async_computation.3 | async-start | bytes 1048576 | tf_op jit(solution)/shard_map/psum | solution.py:102
  214.9 8.8 %copy-start = (bf16[320,16,128]{2,0,1:T(8,128)(2,1)}, bf16[320,16,128]{2,0,1:T(8,128)(2,1)S(1)}, u32[]{:S(2)}) copy-start(bf16[320,16,128]{2,0,1:T(8,128)(2,1)S(1)} %fusion.114) | copy-start | bytes 3932164
  223.6 2.8 copy-start.5
  226.4 146.6 %all-reduce.14.cloned.1.call-start = ((), (), s32[]{:S(2)}) async-start(), calls=%async_computation.4 | async-start | bytes 524288 | tf_op jit(solution)/shard_map/psum | solution.py:105
  226.4 2.1 copy-start.4
  279.7 2.7 copy-start.3
Sparse Core Ops, SparseCore 0:
  71.5 49.8 all-reduce.5
  145.1 30.1 all-reduce.7
  177.7 35.4 all-reduce.9
  226.5 38.4 all-reduce.11
  282.5 90.4 all-reduce.13
